TPU v7x, 32 devices: a whole 2x2x4 slice. The times are simulated.
32 devices in a mesh: shot: 8 (over z, y), rcv: 4 (over x, core).
Axes of the slice: x: 2, y: 2, z: 4, core: 2. Of those that a mesh axis runs over, the one named last changes fastest.
Arguments:
- records: bfloat16 [1, 2, 1024, 8192], P(None, None, 'shot', 'rcv'), may hold values from -6 to 6
- aperture: int32 [1024, 2], P('shot'), may hold values from 0 to 3, all different within a row
- block_owner: int32 [4], replicated, may hold values from 0 to 7, as said below
- block_receivers: int32 [4, 128], replicated, may hold values from 0 to 8191, as said below
Outputs:
- multiples: bfloat16 [1, 2, 1024, 8192], P(None, None, 'shot', 'rcv')
Inputs may be any that keep to these rules, and one draw needn't show every extreme that they name: `block_owner`: distinct indices. `block_receivers`: distinct receivers.
All inputs are finite; a program needn't handle non-finite values.
Results may differ from a plain program's by a relative error of at most 0.001.
Values may be sent and summed in bfloat16 or wider, within the bound.
No kernel may reach another device: no remote copies, remote signals or barrier semaphores. Data moves between devices by JAX's collectives and lax.ppermute only.
A program may use at most 128 MiB of HBM per device.

v0:
```python
import jax
import jax.numpy as jnp
from jax import lax
from jax.sharding import PartitionSpec as P

APER = 2
BLOCK = 128


def broadcast(value, axis, source):
    kept = jnp.where(lax.axis_index(axis) == source, value, 0).astype(value.dtype)
    return lax.psum(kept, axis)


def complex_terms(block_portion, distant_offset):
    real_component = jnp.einsum(
        "uze,uew->uzw",
        block_portion[:, 0],
        distant_offset[:, 0],
        preferred_element_type=jnp.float32,
    ) - jnp.einsum(
        "uze,uew->uzw",
        block_portion[:, 1],
        distant_offset[:, 1],
        preferred_element_type=jnp.float32,
    )
    imag_part = jnp.einsum(
        "uze,uew->uzw",
        block_portion[:, 0],
        distant_offset[:, 1],
        preferred_element_type=jnp.float32,
    ) + jnp.einsum(
        "uze,uew->uzw",
        block_portion[:, 1],
        distant_offset[:, 0],
        preferred_element_type=jnp.float32,
    )
    return (real_component, imag_part)


def per_device(records, aperture, block_owner, block_receivers):
    freqs, parts, shots_here, rcv_here = records.shape
    nblocks, block_extent = block_receivers.shape
    first_rcv = lax.axis_index("rcv") * rcv_here
    requested_rows = block_receivers.reshape(1, -1)
    column_ids = first_rcv + lax.broadcasted_iota(jnp.int32, (rcv_here, 1), 0)
    selector = (column_ids == requested_rows).astype(jnp.bfloat16)
    local_cols = jnp.einsum("fcsr,rx->fcsx", records, selector, preferred_element_type=jnp.float32)
    near = lax.psum(local_cols.astype(jnp.bfloat16), "rcv")
    blocks = lax.broadcasted_iota(jnp.int32, (1, 1, nblocks), 2)
    use = jnp.any(aperture[:, :, None] == blocks, axis=1).astype(jnp.bfloat16)
    masked = (
        near.reshape(freqs, parts, shots_here, nblocks, block_extent) * use[None, None, :, :, None]
    )
    masked = masked.reshape(freqs, parts, shots_here, nblocks * block_extent)

    def fetch(block):
        return broadcast(records, "shot", block_owner[block])

    real_total = jnp.zeros((freqs, shots_here, rcv_here), jnp.float32)
    imaginary_total = jnp.zeros((freqs, shots_here, rcv_here), jnp.float32)
    gathered_rows = [fetch(block) for block in range(nblocks)]
    for block in range(nblocks):
        block_portion = masked[:, :, :, block * block_extent : (block + 1) * block_extent]
        real_component, imag_part = complex_terms(block_portion, gathered_rows[block])
        real_total = real_total + real_component
        imaginary_total = imaginary_total + imag_part
    factor = (2.0 * APER * BLOCK) ** (-0.5)
    return (jnp.stack([real_total, imaginary_total], axis=1) * factor).astype(jnp.bfloat16)


def solution(mesh):
    placed = (P(None, None, "shot", "rcv"), P("shot", None), P(), P())
    return jax.shard_map(
        per_device,
        mesh=mesh,
        in_specs=placed,
        out_specs=P(None, None, "shot", "rcv"),
        check_vma=False,
    )
```

profile of v0, /device:TPU:0, one launch (start us, length us, event | category | flops | bytes accessed | tf_op | source)
XLA Modules:
  0.0 222.4 jit_solution(10446118807844659125)
XLA Ops:
  6.6 2.8 %fusion.17 = bf16[1,2,128,512]{2,3,1,0:T(8,128)(2,1)} fusion(s32[2048]{0:T(1024)S(1)} %iota_add_fusion, s32[512]{0:T(512)} %bitcast.89, bf16[1,2,128,2048]{3,2,1,0:T(8,128)(2,1)} %param.4), kind=kOutput, calls=%fused_computation.24 | convolution fusion | flops 538050560 | bytes 1320960 | tf_op jit(solution)/shard_map/fcsr,rx->fcsx/dot_general | solution.py:48
  9.4 0.7 fusion.30
  12.7 2.1 broadcast_select_fusion
  14.8 0.7 copy-done.6
  15.5 29.2 %all-reduce.4.cloned.1.call-done = bf16[1,2,128,512]{2,3,1,0:T(8,128)(2,1)} async-done(((bf16[1,2,128,512]{2,3,1,0:T(8,128)(2,1)}), bf16[1,2,128,512]{2,3,1,0:T(8,128)(2,1)}) %all-reduce.4.cloned.1.call-update) | async-done | bytes 262160 | tf_op jit(solution)/shard_map/psum | solution.py:49
  44.7 1.0 broadcast_multiply_fusion
  45.7 159.6 %all-reduce.6.cloned.1.call-done = (bf16[1,2,128,2048]{3,2,1,0:T(8,128)(2,1)}, bf16[1,2,128,2048]{3,2,1,0:T(8,128)(2,1)}, bf16[1,2,128,2048]{3,2,1,0:T(8,128)(2,1)}, bf16[1,2,128,2048]{3,2,1,0:T(8,128)(2,1)}) async-done(((bf16[1,2,128,2048]{3,2,1,0:T(8,128)(2,1)}, bf16[1,2,128,2048]{3,2,1,0:T(8,128)(2,1)}, bf16[1,2,128,2048]{3,2,1,0:T(8,128)(2,1)}, bf16[1,2,128,2048]{3,2,1,0:T(8,128)(2,1)}), ...) | async-done | bytes 4194320 | tf_op jit(solution)/shard_map/psum | solution.py:12
  205.3 1.4 fusion.21
  206.7 0.3 fusion.22
  207.1 0.9 copy-done.2
  208.0 0.3 fusion.23
  208.6 0.9 copy-done.1
  209.5 0.3 fusion.25
  210.2 0.9 copy-done
  211.1 0.3 fusion.27
  211.7 0.3 convolution_subtract_fusion.3
  212.0 0.3 convolution_add_fusion.3
  212.4 0.3 fusion.10
  212.7 0.3 fusion.9
  213.1 0.3 fusion.8
  213.4 0.3 fusion.6
  213.7 0.3 fusion.5
  214.1 0.3 fusion.4
  214.4 1.2 fusion.11
  (21 shorter events, 1.1 us)
Async XLA Ops:
  6.5 38.2 %all-reduce.4.cloned.1.call-start = ((), (), s32[]{:S(2)}) async-start(), calls=%async_computation | async-start | bytes 524288 | tf_op jit(solution)/shard_map/psum | solution.py:49
  6.5 2.9 %copy-start.5 = (s32[4]{0:T(128)S(1)}, s32[4]{0:T(128)}, u32[]{:S(2)}) copy-start(s32[4]{0:T(128)} %param.6) | copy-start | bytes 52
  6.5 6.2 %copy-start.4 = (bf16[1,2,128,2048]{3,2,1,0:T(8,128)(2,1)S(1)}, bf16[1,2,128,2048]{3,2,1,0:T(8,128)(2,1)}, u32[]{:S(2)}) copy-start(bf16[1,2,128,2048]{3,2,1,0:T(8,128)(2,1)} %param.4) | copy-start | bytes 3145732
  9.4 195.9 %all-reduce.6.cloned.1.call-start = ((), (), s32[]{:S(2)}) async-start(), calls=%async_computation.1 | async-start | bytes 8388608 | tf_op jit(solution)/shard_map/psum | solution.py:12
  14.8 0.7 copy-start.6
  205.3 1.5 copy-start.3
  206.7 1.2 copy-start.2
  208.3 1.2 copy-start.1
  209.8 1.2 copy-start
Sparse Core Ops, SparseCore 0:
  9.7 34.9 all-reduce.3
  48.7 156.4 all-reduce.5
where the time goes:
time: 223 us; the launch traced here: 222 us
  waiting for transfers between devices  189 us (85%)
  between operations  16.1 us (7%)
  matrix products  9.14 us (4%)
  other arithmetic  4.27 us (2%)
  local copies, waits for them, and re-layouts  4.04 us (2%)
    psum x1, waiting for transfers between devices, broadcast(): return lax.psum(kept, axis)  160 us
    psum x1, waiting for transfers between devices, per_device(): near = lax.psum(local_cols.astype(jnp.bfloat16), 'rcv')  29.2 us
  transfers between devices with their start and end apart: 2, of which 2 were waited for; matrix products, arithmetic and copies ran while one was open for 2% of the time, Pallas kernels for 0%

commit v1 on v0

--- a/solution.py
+++ b/solution.py
@@ -8,8 +8,13 @@
 
 
 def broadcast(value, axis, source):
+
+    def _cover_heaps(inp, ax_name):
+        newest = lax.all_gather(inp, axis_name=ax_name).sum(axis=0)
+        return newest
+
     kept = jnp.where(lax.axis_index(axis) == source, value, 0).astype(value.dtype)
-    return lax.psum(kept, axis)
+    return _cover_heaps(kept, axis)
 
 
 def complex_terms(block_portion, distant_offset):

time: 223 us -> 537 us (2.41)
  waiting for transfers between devices: 189 us -> 475 us
  other arithmetic: 4.27 us -> 25.1 us
  matrix products: 9.14 us -> 15.7 us
    all_gather x0 -> x4, waiting for transfers between devices: none -> 447 us  [_cover_heaps(): newest = lax.all_gather(inp, axis_name=ax_name).sum(axis=0)]
    psum x1 -> x0, waiting for transfers between devices: 160 us -> none  [broadcast(): return lax.psum(kept, axis)]
    reduce_sum x0 -> x4, other arithmetic: none -> 20.9 us  [_cover_heaps(): newest = lax.all_gather(inp, axis_name=ax_name).sum(axis=0)]
  transfers between devices with their start and end apart: 2 -> 5, of which waited for: 2 -> 5; matrix products, arithmetic and copies ran while one was open for 2% -> 5% of each run, Pallas kernels for 0% -> 0%
where the time goes in v1:
time: 537 us; the launch traced here: 536 us
  waiting for transfers between devices  475 us (88%)
  other arithmetic  25.1 us (5%)
  between operations  17.9 us (3%)
  matrix products  15.7 us (3%)
    all_gather x4, waiting for transfers between devices, _cover_heaps(): newest = lax.all_gather(inp, axis_name=ax_name).sum(axis=0)  447 us
    psum x1, waiting for transfers between devices, per_device(): near = lax.psum(local_cols.astype(jnp.bfloat16), 'rcv')  27.1 us
    reduce_sum x4, other arithmetic, _cover_heaps(): newest = lax.all_gather(inp, axis_name=ax_name).sum(axis=0)  20.9 us
  transfers between devices with their start and end apart: 5, of which 5 were waited for; matrix products, arithmetic and copies ran while one was open for 5% of the time, Pallas kernels for 0%

profile of v1, /device:TPU:0, one launch (start us, length us, event | category | flops | bytes accessed | tf_op | source)
XLA Modules:
  0.0 536.4 jit_solution(2586172083104466017)
XLA Ops:
  7.4 2.8 fusion.17
  10.3 1.5 fusion.30
  14.3 2.1 broadcast_select_fusion
  16.5 0.5 all-gather.9.cloned.1.call-update
  17.1 0.5 all-gather.13.cloned.1.call-update
  17.7 0.7 all-gather.15.cloned.1.call-update
  18.4 27.1 %all-reduce.2.cloned.1.call-done = bf16[1,2,128,512]{2,3,1,0:T(8,128)(2,1)} async-done(((bf16[1,2,128,512]{2,3,1,0:T(8,128)(2,1)}), bf16[1,2,128,512]{2,3,1,0:T(8,128)(2,1)}) %all-reduce.2.cloned.1.call-update) | async-done | bytes 262160 | tf_op jit(solution)/shard_map/psum | solution.py:54
  45.5 1.0 broadcast_multiply_fusion
  46.5 96.9 %all-gather.11.cloned.1.call-done = bf16[8,2,128,2048]{3,2,1,0:T(8,128)(2,1)} async-done(((bf16[1,2,128,2048]{3,2,1,0:T(8,128)(2,1)}), bf16[8,2,128,2048]{3,2,1,0:T(8,128)(2,1)}) %all-gather.11.cloned.1.call-update) | async-done | bytes 8388624 | tf_op jit(solution)/shard_map/all_gather | solution.py:13
  143.5 5.2 reduce.9
  148.7 119.1 %all-gather.9.cloned.1.call-done = bf16[8,2,128,2048]{3,2,1,0:T(8,128)(2,1)} async-done(((bf16[1,2,128,2048]{3,2,1,0:T(8,128)(2,1)}), bf16[8,2,128,2048]{3,2,1,0:T(8,128)(2,1)}) %all-gather.9.cloned.1.call-update) | async-done | bytes 8388624 | tf_op jit(solution)/shard_map/all_gather | solution.py:13
  267.8 5.2 reduce.8
  273.0 119.1 %all-gather.13.cloned.1.call-done = bf16[8,2,128,2048]{3,2,1,0:T(8,128)(2,1)} async-done(((bf16[1,2,128,2048]{3,2,1,0:T(8,128)(2,1)}), bf16[8,2,128,2048]{3,2,1,0:T(8,128)(2,1)}) %all-gather.13.cloned.1.call-update) | async-done | bytes 8388624 | tf_op jit(solution)/shard_map/all_gather | solution.py:13
  392.2 5.2 reduce.10
  397.4 1.3 fusion.26
  398.7 1.4 fusion.25
  400.1 1.3 fusion.22
  401.4 1.4 fusion.21
  402.7 1.3 fusion.24
  404.1 1.3 fusion.23
  405.4 111.3 %all-gather.15.cloned.1.call-done = bf16[8,2,128,2048]{3,2,1,0:T(8,128)(2,1)} async-done(((bf16[1,2,128,2048]{3,2,1,0:T(8,128)(2,1)}), bf16[8,2,128,2048]{3,2,1,0:T(8,128)(2,1)}) %all-gather.15.cloned.1.call-update) | async-done | bytes 8388624 | tf_op jit(solution)/shard_map/all_gather | solution.py:13
  516.7 5.2 reduce.11
  522.6 2.0 convolution_add_fusion.3
  527.6 1.2 fusion.11
  (38 shorter events, 3.9 us)
Async XLA Ops:
  7.4 6.9 %copy-start.7 = (bf16[1,2,128,2048]{3,2,1,0:T(8,128)(2,1)S(1)}, bf16[1,2,128,2048]{3,2,1,0:T(8,128)(2,1)}, u32[]{:S(2)}) copy-start(bf16[1,2,128,2048]{3,2,1,0:T(8,128)(2,1)} %param.4) | copy-start | bytes 3145732
  7.4 38.2 %all-reduce.2.cloned.1.call-start = ((), (), s32[]{:S(2)}) async-start(), calls=%async_computation | async-start | bytes 524288 | tf_op jit(solution)/shard_map/psum | solution.py:54
  10.2 133.3 %all-gather.11.cloned.1.call-start = ((), (), s32[]{:S(2)}) async-start(), calls=%async_computation.2 | async-start | bytes 9437184 | tf_op jit(solution)/shard_map/all_gather | solution.py:13
  14.3 4.0 copy-start.8
  16.5 251.4 %all-gather.9.cloned.1.call-start = ((), (), s32[]{:S(2)}) async-start(), calls=%async_computation.1 | async-start | bytes 9437184 | tf_op jit(solution)/shard_map/all_gather | solution.py:13
  17.1 375.1 %all-gather.13.cloned.1.call-start = ((), (), s32[]{:S(2)}) async-start(), calls=%async_computation.3 | async-start | bytes 9437184 | tf_op jit(solution)/shard_map/all_gather | solution.py:13
  17.6 499.1 %all-gather.15.cloned.1.call-start = ((), (), s32[]{:S(2)}) async-start(), calls=%async_computation.4 | async-start | bytes 9437184 | tf_op jit(solution)/shard_map/all_gather | solution.py:13
  273.0 128.3 %copy-start = (bf16[2,128,2048]{2,1,0:T(8,128)(2,1)}, bf16[2,128,2048]{2,1,0:T(8,128)(2,1)S(1)}, u32[]{:S(2)}) copy-start(bf16[2,128,2048]{2,1,0:T(8,128)(2,1)S(1)} %reduce.8) | copy-start | bytes 3145732
  521.9 2.7 copy-start.1
  521.9 2.7 copy-start.6
  521.9 3.0 copy-start.5
  522.6 2.7 copy-start.3
  524.9 1.2 copy-start.4
  525.3 1.3 copy-start.2
Sparse Core Ops, SparseCore 0:
  10.5 34.9 all-reduce.1
Sparse Core Ops, SparseCore 1:
  16.5 126.9 all-gather.10
  145.5 122.3 all-gather.8
  269.8 122.3 all-gather.12
  394.3 122.3 all-gather.14
